TPU v7x, 32 devices: a whole 2x2x4 slice. The times are simulated.
32 devices in a mesh: grp: 4 (over x, core), ep: 8 (over z, y).
Axes of the slice: x: 2, y: 2, z: 4, core: 2. Of those that a mesh axis runs over, the one named last changes fastest.
Arguments:
- tokens: bfloat16 [2048, 5120], P('ep', 'grp'), may hold values from -6 to 6
- cotangent: bfloat16 [2048, 5120], P('ep', 'grp'), may hold values from -0.59765625 to 0.59765625
- gate_weights: bfloat16 [2048, 6], P('ep'), may hold values from 0.099609375 to 1
- expert_ids: int32 [2048, 6], P('ep'), may hold values from 0 to 159, all different within a row; in each aligned block of 256 rows (0 to 255, 256 to 511, ...) at most 16 rows name the same one
- hot_ids: int32 [2], replicated, may hold values from 8 to 159, as said below
- gate_cold: bfloat16 [8, 5120, 768], P('ep', 'grp'), may hold values from -0.078125 to 0.078125
- up_cold: bfloat16 [8, 5120, 768], P('ep', 'grp'), may hold values from -0.078125 to 0.078125
- down_cold: bfloat16 [8, 768, 5120], P('ep', None, 'grp'), may hold values from -0.21875 to 0.21875
- gate_hot: bfloat16 [2, 5120, 768], P(None, 'grp', 'ep'), may hold values from -0.078125 to 0.078125
- up_hot: bfloat16 [2, 5120, 768], P(None, 'grp', 'ep'), may hold values from -0.078125 to 0.078125
- down_hot: bfloat16 [2, 768, 5120], P(None, 'ep', 'grp'), may hold values from -0.21875 to 0.21875
Outputs:
- grad_gate_cold: bfloat16 [8, 5120, 768], P('ep', 'grp')
- grad_up_cold: bfloat16 [8, 5120, 768], P('ep', 'grp')
- grad_down_cold: bfloat16 [8, 768, 5120], P('ep', None, 'grp')
- grad_gate_hot: float32 [2, 5120, 768], P(None, 'grp', 'ep')
- grad_up_hot: float32 [2, 5120, 768], P(None, 'grp', 'ep')
- grad_down_hot: float32 [2, 768, 5120], P(None, 'ep', 'grp')
- gate_weight_grad: float32 [2048, 6], P('ep')
Inputs may be any that keep to these rules, and one draw needn't show every extreme that they name: `expert_ids`: each row names 6 different experts. Among the routes of the 256 tokens of one index of ep (aligned blocks of rows) no expert is named more than 16 times, a bound that some block reaches. `hot_ids`: distinct expert numbers, none below 8; expert 160 - 1 is always among them.
All inputs are finite; a program needn't handle non-finite values.
Results may differ from a plain program's by a relative error of at most 0.02.
Values may be sent and summed in bfloat16 or wider, within the bound.
No kernel may reach another device: no remote copies, remote signals or barrier semaphores. Data moves between devices by JAX's collectives and lax.ppermute only.
A program may use at most 128 MiB of HBM per device.

v0:
```python
import jax
import jax.numpy as jnp
from jax import lax
from jax.sharding import PartitionSpec as P


def route_table(flat_ids, targets, capacity):
    matches = (flat_ids[:, None] == targets[None, :]).astype(jnp.int32)
    rank_of = jnp.cumsum(matches, axis=0) - 1
    slot_of = jnp.sum(matches * rank_of, axis=1)
    owner_of = jnp.sum(matches * jnp.arange(targets.shape[0], dtype=jnp.int32)[None, :], axis=1)
    usable = jnp.sum(matches, axis=1) > 0
    row_of = owner_of * capacity + slot_of
    rows_total = targets.shape[0] * capacity
    route_map = (row_of[None, :] == jnp.arange(rows_total, dtype=jnp.int32)[:, None]) & usable[
        None, :
    ]
    return route_map.astype(jnp.float32)


def gather_rows(route_map, tokens, cotangent, flat_weights, tok_rows, top_count):
    per_token = jnp.sum(route_map.reshape(route_map.shape[0], tok_rows, top_count), axis=2)
    token_map = per_token.astype(jnp.bfloat16)
    feat_rows = jnp.dot(token_map, tokens, preferred_element_type=jnp.float32).astype(jnp.bfloat16)
    cotan_rows = jnp.dot(token_map, cotangent, preferred_element_type=jnp.float32).astype(
        jnp.bfloat16
    )
    scale_rows = jnp.dot(
        route_map, flat_weights.astype(jnp.float32), precision=lax.Precision.HIGHEST
    )
    return (feat_rows, cotan_rows, scale_rows.astype(jnp.bfloat16))


def swiglu_back(pre_gate, pre_up, grad_hidden):
    sigmoid_gate = jax.nn.sigmoid(pre_gate)
    activated = pre_gate * sigmoid_gate
    hidden = (activated * pre_up).astype(jnp.bfloat16)
    back_gate = (
        grad_hidden * pre_up * sigmoid_gate * (1.0 + pre_gate * (1.0 - sigmoid_gate))
    ).astype(jnp.bfloat16)
    back_up = (grad_hidden * activated).astype(jnp.bfloat16)
    return (hidden, back_gate, back_up)


def body(
    tokens,
    cotangent,
    gate_weights,
    expert_ids,
    hot_ids,
    gate_cold,
    up_cold,
    down_cold,
    gate_hot,
    up_hot,
    down_hot,
):
    tok_rows, slice_width = tokens.shape
    top_count = expert_ids.shape[1]
    cold_count = lax.axis_size("ep")
    hot_count = hot_ids.shape[0]
    capacity = tok_rows // 16
    flat_ids = expert_ids.reshape(-1)
    flat_weights = gate_weights.reshape(-1)
    cold_map = route_table(flat_ids, jnp.arange(cold_count, dtype=jnp.int32), capacity)
    hot_map = route_table(flat_ids, hot_ids, capacity)
    cold_feats, cold_cotan, cold_scale = gather_rows(
        cold_map, tokens, cotangent, flat_weights, tok_rows, top_count
    )
    hot_feats, hot_cotan, hot_scale = gather_rows(
        hot_map, tokens, cotangent, flat_weights, tok_rows, top_count
    )
    outgoing = (
        cold_feats.reshape(cold_count, capacity, slice_width),
        cold_cotan.reshape(cold_count, capacity, slice_width),
        cold_scale.reshape(cold_count, capacity),
    )
    recv_feats, recv_cotan, recv_scale = (
        lax.all_to_all(outgoing[0], "ep", split_axis=0, concat_axis=0, tiled=True),
        lax.all_to_all(outgoing[1], "ep", split_axis=0, concat_axis=0, tiled=True),
        lax.all_to_all(outgoing[2], "ep", split_axis=0, concat_axis=0, tiled=True),
    )
    recv_feats = recv_feats.reshape(-1, slice_width)
    recv_cotan = recv_cotan.reshape(-1, slice_width)
    weighted = (
        recv_scale.reshape(-1).astype(jnp.float32)[:, None] * recv_cotan.astype(jnp.float32)
    ).astype(jnp.bfloat16)
    w_gate = gate_cold[0]
    w_up = up_cold[0]
    w_down = down_cold[0]
    part_gate = jnp.dot(recv_feats, w_gate, preferred_element_type=jnp.float32)
    part_up = jnp.dot(recv_feats, w_up, preferred_element_type=jnp.float32)
    part_hidden = lax.dot_general(
        weighted, w_down, (((1,), (1,)), ((), ())), preferred_element_type=jnp.float32
    )
    pre_gate, pre_up, grad_hidden = (
        lax.psum(part_gate.astype(jnp.bfloat16), "grp").astype(jnp.float32),
        lax.psum(part_up.astype(jnp.bfloat16), "grp").astype(jnp.float32),
        lax.psum(part_hidden.astype(jnp.bfloat16), "grp").astype(jnp.float32),
    )
    hidden, back_gate, back_up = swiglu_back(pre_gate, pre_up, grad_hidden)
    output_slice = jnp.dot(hidden, w_down, preferred_element_type=jnp.float32)
    cold_route = jnp.sum(output_slice * recv_cotan.astype(jnp.float32), axis=1)
    contract_rows = (((0,), (0,)), ((), ()))
    grad_gate_cold = lax.dot_general(
        recv_feats, back_gate, contract_rows, preferred_element_type=jnp.float32
    )
    grad_up_cold = lax.dot_general(
        recv_feats, back_up, contract_rows, preferred_element_type=jnp.float32
    )
    grad_down_cold = lax.dot_general(
        hidden, weighted, contract_rows, preferred_element_type=jnp.float32
    )
    hot_feats = hot_feats.reshape(hot_count, capacity, slice_width)
    hot_cotan = hot_cotan.reshape(hot_count, capacity, slice_width)
    hot_scale = hot_scale.reshape(hot_count, capacity)
    full_gate, full_up = (
        lax.all_gather(gate_hot, "ep", axis=2, tiled=True),
        lax.all_gather(up_hot, "ep", axis=2, tiled=True),
    )
    full_down = lax.all_gather(down_hot, "ep", axis=1, tiled=True)
    hot_weighted = (
        hot_scale.astype(jnp.float32)[:, :, None] * hot_cotan.astype(jnp.float32)
    ).astype(jnp.bfloat16)
    part_gate_hot = jnp.einsum(
        "jcd,jdh->jch", hot_feats, full_gate, preferred_element_type=jnp.float32
    )
    part_up_hot = jnp.einsum("jcd,jdh->jch", hot_feats, full_up, preferred_element_type=jnp.float32)
    part_hidden_hot = jnp.einsum(
        "jcd,jhd->jch", hot_weighted, full_down, preferred_element_type=jnp.float32
    )
    pre_gate_hot, pre_up_hot, grad_hidden_hot = (
        lax.psum(part_gate_hot.astype(jnp.bfloat16), "grp").astype(jnp.float32),
        lax.psum(part_up_hot.astype(jnp.bfloat16), "grp").astype(jnp.float32),
        lax.psum(part_hidden_hot.astype(jnp.bfloat16), "grp").astype(jnp.float32),
    )
    hidden_hot, back_gate_hot, back_up_hot = swiglu_back(pre_gate_hot, pre_up_hot, grad_hidden_hot)
    output_hot = jnp.einsum(
        "jch,jhd->jcd", hidden_hot, full_down, preferred_element_type=jnp.float32
    )
    hot_route_part = jnp.sum(output_hot * hot_cotan.astype(jnp.float32), axis=2)
    shadow_gate = jnp.einsum(
        "jcd,jch->jdh", hot_feats, back_gate_hot, preferred_element_type=jnp.float32
    )
    shadow_up = jnp.einsum(
        "jcd,jch->jdh", hot_feats, back_up_hot, preferred_element_type=jnp.float32
    )
    shadow_down = jnp.einsum(
        "jch,jcd->jdh", hidden_hot, hot_weighted, preferred_element_type=jnp.float32
    )
    grad_gate_hot, grad_up_hot, down_turned = (
        lax.psum_scatter(
            shadow_gate.astype(jnp.bfloat16), "ep", scatter_dimension=2, tiled=True
        ).astype(jnp.float32),
        lax.psum_scatter(
            shadow_up.astype(jnp.bfloat16), "ep", scatter_dimension=2, tiled=True
        ).astype(jnp.float32),
        lax.psum_scatter(
            shadow_down.astype(jnp.bfloat16), "ep", scatter_dimension=2, tiled=True
        ).astype(jnp.float32),
    )
    grad_down_hot = jnp.transpose(down_turned, (0, 2, 1))
    cold_route, hot_route = lax.psum((cold_route, hot_route_part), "grp")
    cold_back = lax.all_to_all(
        cold_route.reshape(cold_count, capacity), "ep", split_axis=0, concat_axis=0, tiled=True
    )
    route_flat = jnp.dot(cold_back.reshape(-1), cold_map, precision=lax.Precision.HIGHEST)
    route_flat = route_flat + jnp.dot(
        hot_route.reshape(-1), hot_map, precision=lax.Precision.HIGHEST
    )
    gate_weight_grad = route_flat.reshape(tok_rows, top_count)
    return (
        grad_gate_cold[None].astype(jnp.bfloat16),
        grad_up_cold[None].astype(jnp.bfloat16),
        grad_down_cold[None].astype(jnp.bfloat16),
        grad_gate_hot,
        grad_up_hot,
        grad_down_hot,
        gate_weight_grad,
    )


def solution(mesh):
    in_specs = (
        P("ep", "grp"),
        P("ep", "grp"),
        P("ep", None),
        P("ep", None),
        P(),
        P("ep", "grp", None),
        P("ep", "grp", None),
        P("ep", None, "grp"),
        P(None, "grp", "ep"),
        P(None, "grp", "ep"),
        P(None, "ep", "grp"),
    )
    out_specs = (
        P("ep", "grp", None),
        P("ep", "grp", None),
        P("ep", None, "grp"),
        P(None, "grp", "ep"),
        P(None, "grp", "ep"),
        P(None, "ep", "grp"),
        P("ep", None),
    )
    return jax.shard_map(body, mesh=mesh, in_specs=in_specs, out_specs=out_specs, check_vma=False)
```

profile of v0, /device:TPU:0, one launch (start us, length us, event | category | flops | bytes accessed | tf_op | source)
XLA Modules:
  0.0 574.7 jit_solution(6589414462695450256)
XLA Ops:
  14.0 2.3 reduce-window.14
  17.9 7.3 %all-to-all-start.1 = ((bf16[8,1,16]{2,1,0:T(2,128)(2,1)}), bf16[8,1,16]{2,1,0:T(2,128)(2,1)S(1)}, u32[]{:S(2)}, u32[]{:S(2)}) async-start(bf16[8,1,16]{2,1,0:T(2,128)(2,1)} %all_to_all.24), calls=%async_computation.1 | async-start | bytes 8192 | tf_op jit(solution)/shard_map/all_to_all | solution.py:81
  33.5 6.0 %all-to-all-start = ((bf16[8,16,1280]{2,1,0:T(8,128)(2,1)}), bf16[8,16,1280]{2,1,0:T(8,128)(2,1)S(1)}, u32[]{:S(2)}, u32[]{:S(2)}) async-start(bf16[8,16,1280]{2,1,0:T(8,128)(2,1)} %bitcast.121), calls=%async_computation | async-start | bytes 655360 | tf_op jit(solution)/shard_map/all_to_all | solution.py:79
  40.7 11.0 %all-to-all-done = bf16[8,16,1280]{2,1,0:T(8,128)(2,1)S(1)} async-done(((bf16[8,16,1280]{2,1,0:T(8,128)(2,1)}), bf16[8,16,1280]{2,1,0:T(8,128)(2,1)S(1)}, u32[]{:S(2)}, u32[]{:S(2)}) %all-to-all-start) | async-done | bytes 327712 | tf_op jit(solution)/shard_map/all_to_all | solution.py:79
  51.8 5.0 all-to-all-start.2
  56.8 2.7 fusion.16
  59.4 2.7 fusion.19
  62.1 13.3 %all-to-all-done.2 = bf16[8,16,1280]{2,1,0:T(8,128)(2,1)S(1)} async-done(((bf16[8,16,1280]{2,1,0:T(8,128)(2,1)}), bf16[8,16,1280]{2,1,0:T(8,128)(2,1)S(1)}, u32[]{:S(2)}, u32[]{:S(2)}) %all-to-all-start.2) | async-done | bytes 327712 | tf_op jit(solution)/shard_map/all_to_all | solution.py:80
  75.5 12.9 %all-gather.8.cloned.1.call-done = bf16[2,1280,768]{1,2,0:T(8,128)(2,1)} async-done(((bf16[2,1280,96]{1,2,0:T(8,128)(2,1)}), bf16[2,1280,768]{1,2,0:T(8,128)(2,1)}) %all-gather.8.cloned.1.call-update) | async-done | bytes 3932176 | tf_op jit(solution)/shard_map/all_gather | solution.py:118
  88.4 3.9 convolution_convert_fusion.10
  92.3 67.5 %all-gather.6.cloned.1.call-done = bf16[2,1280,768]{1,2,0:T(8,128)(2,1)} async-done(((bf16[2,1280,96]{1,2,0:T(8,128)(2,1)}), bf16[2,1280,768]{1,2,0:T(8,128)(2,1)}) %all-gather.6.cloned.1.call-update) | async-done | bytes 3932176 | tf_op jit(solution)/shard_map/all_gather | solution.py:119
  159.7 3.9 convolution_convert_fusion.11
  163.6 66.8 %all-gather.4.cloned.1.call-done = bf16[2,768,1280]{2,1,0:T(8,128)(2,1)} async-done(((bf16[2,96,1280]{2,1,0:T(8,128)(2,1)}), bf16[2,768,1280]{2,1,0:T(8,128)(2,1)}) %all-gather.4.cloned.1.call-update) | async-done | bytes 3932176 | tf_op jit(solution)/shard_map/all_gather | solution.py:121
  230.4 3.9 convolution_convert_fusion.12
  235.9 27.8 %all-reduce.6.cloned.1.call-done = (bf16[2,16,768]{2,1,0:T(8,128)(2,1)}, bf16[2,16,768]{2,1,0:T(8,128)(2,1)}, bf16[2,16,768]{2,1,0:T(8,128)(2,1)}) async-done(((bf16[2,16,768]{2,1,0:T(8,128)(2,1)}, bf16[2,16,768]{2,1,0:T(8,128)(2,1)}, bf16[2,16,768]{2,1,0:T(8,128)(2,1)}), (bf16[2,16,768]{2,1,0:T(8,128)(2,1)}, bf16[2,16,768]{2,1,0:T(8,128)(2,1)}, bf16[2,16,768]{2,1,0:T(8,128)(2,1)})) %all-reduce.6.cloned.1.call-update) | async-done | bytes 147472 | tf_op jit(solution)/shard_map/psum | solution.py:134
  263.8 4.0 convolution_convert_fusion.1
  267.9 3.2 convolution_convert_fusion
  271.4 3.2 convolution_convert_fusion.2
  274.8 26.7 %all-reduce.8.cloned.1.call-done = (bf16[128,768]{1,0:T(8,128)(2,1)}, bf16[128,768]{1,0:T(8,128)(2,1)}, bf16[128,768]{1,0:T(8,128)(2,1)}) async-done(((bf16[128,768]{1,0:T(8,128)(2,1)}, bf16[128,768]{1,0:T(8,128)(2,1)}, bf16[128,768]{1,0:T(8,128)(2,1)}), (bf16[128,768]{1,0:T(8,128)(2,1)}, bf16[128,768]{1,0:T(8,128)(2,1)}, bf16[128,768]{1,0:T(8,128)(2,1)})) %all-reduce.8.cloned.1.call-update) | async-done | bytes 589840 | tf_op jit(solution)/shard_map/psum | solution.py:98
  301.5 1.6 fusion.10
  303.3 2.0 fusion.2
  305.3 2.9 fusion.1
  308.2 2.0 fusion
  311.0 6.4 %all-reduce = (f32[8,1,16]{2,0,1:T(8,128)}, f32[32]{0:T(128)S(1)}) all-reduce(f32[8,1,16]{2,0,1:T(8,128)S(1)} %all_to_all.22, f32[32]{0:T(128)S(1)} %reshape.191), channel_id=1, replica_groups=mesh['grp'=4,'ep'=8] {'grp'}, use_global_device_ids=true, to_apply=%region_22.23 | all-reduce | flops 160 | bytes 1280 | tf_op jit(solution)/shard_map/psum | solution.py:163
  317.4 5.8 %all-to-all-start.3 = ((f32[8,1,16]{2,1,0:T(1,128)}), f32[8,1,16]{2,1,0:T(1,128)S(1)}, u32[]{:S(2)}, u32[]{:S(2)}) async-start(f32[8,1,16]{2,1,0:T(1,128)} %bitcast.19), calls=%async_computation.6 | async-start | bytes 8192 | tf_op jit(solution)/shard_map/all_to_all | solution.py:164
  323.5 6.4 %all-to-all-done.3 = f32[8,1,16]{2,1,0:T(1,128)S(1)} async-done(((f32[8,1,16]{2,1,0:T(1,128)}), f32[8,1,16]{2,1,0:T(1,128)S(1)}, u32[]{:S(2)}, u32[]{:S(2)}) %all-to-all-start.3) | async-done | bytes 544 | tf_op jit(solution)/shard_map/all_to_all | solution.py:164
  332.4 57.6 %reduce-scatter.6.cloned.1.call-done = bf16[2,1280,96]{1,2,0:T(8,128)(2,1)} async-done(((bf16[2,1280,768]{1,2,0:T(8,128)(2,1)}), bf16[2,1280,96]{1,2,0:T(8,128)(2,1)}) %reduce-scatter.6.cloned.1.call-update) | async-done | bytes 491536 | tf_op jit(solution)/shard_map/reduce_scatter | solution.py:155
  390.0 2.0 convert_element_type.245
  392.0 85.7 %reduce-scatter.8.cloned.1.call-done = bf16[2,1280,96]{1,2,0:T(8,128)(2,1)} async-done(((bf16[2,1280,768]{1,2,0:T(8,128)(2,1)}), bf16[2,1280,96]{1,2,0:T(8,128)(2,1)}) %reduce-scatter.8.cloned.1.call-update) | async-done | bytes 491536 | tf_op jit(solution)/shard_map/reduce_scatter | solution.py:158
  477.7 2.0 convert_bitcast_fusion
  479.7 86.1 %reduce-scatter.4.cloned.1.call-done = bf16[2,1280,96]{1,2,0:T(8,128)(2,1)} async-done(((bf16[2,1280,768]{1,2,0:T(8,128)(2,1)}), bf16[2,1280,96]{1,2,0:T(8,128)(2,1)}) %reduce-scatter.4.cloned.1.call-update) | async-done | bytes 491536 | tf_op jit(solution)/shard_map/reduce_scatter | solution.py:152
  565.9 2.0 convert_element_type.242
  (91 shorter events, 23.6 us)
Async XLA Ops:
  7.2 227.2 %copy-start = (bf16[1,768,1280]{2,1,0:T(8,128)(2,1)S(1)}, bf16[1,768,1280]{2,1,0:T(8,128)(2,1)}, u32[]{:S(2)}) copy-start(bf16[1,768,1280]{2,1,0:T(8,128)(2,1)} %param.18) | copy-start | bytes 5898244
  7.2 24.8 %copy-start.2 = (bf16[256,1280]{1,0:T(8,128)(2,1)S(1)}, bf16[256,1280]{1,0:T(8,128)(2,1)}, u32[]{:S(2)}) copy-start(bf16[256,1280]{1,0:T(8,128)(2,1)} %param.11) | copy-start | bytes 1966084
  7.2 26.1 %copy-start.3 = (bf16[256,1280]{1,0:T(8,128)(2,1)S(1)}, bf16[256,1280]{1,0:T(8,128)(2,1)}, u32[]{:S(2)}) copy-start(bf16[256,1280]{1,0:T(8,128)(2,1)} %param.12) | copy-start | bytes 1966084
  7.2 81.2 %all-gather.8.cloned.1.call-start = ((), (), s32[]{:S(2)}) async-start(), calls=%async_computation.9 | async-start | bytes 4423680 | tf_op jit(solution)/shard_map/all_gather | solution.py:118
  7.9 151.8 %all-gather.6.cloned.1.call-start = ((), (), s32[]{:S(2)}) async-start(), calls=%async_computation.8 | async-start | bytes 4423680 | tf_op jit(solution)/shard_map/all_gather | solution.py:119
  8.7 221.7 %all-gather.4.cloned.1.call-start = ((), (), s32[]{:S(2)}) async-start(), calls=%async_computation.7 | async-start | bytes 4423680 | tf_op jit(solution)/shard_map/all_gather | solution.py:121
  17.9 15.6 %all-to-all-start.1 = ((bf16[8,1,16]{2,1,0:T(2,128)(2,1)}), bf16[8,1,16]{2,1,0:T(2,128)(2,1)S(1)}, u32[]{:S(2)}, u32[]{:S(2)}) async-start(bf16[8,1,16]{2,1,0:T(2,128)(2,1)} %all_to_all.24), calls=%async_computation.1 | async-start | bytes 8192 | tf_op jit(solution)/shard_map/all_to_all | solution.py:81
  33.5 18.3 %all-to-all-start = ((bf16[8,16,1280]{2,1,0:T(8,128)(2,1)}), bf16[8,16,1280]{2,1,0:T(8,128)(2,1)S(1)}, u32[]{:S(2)}, u32[]{:S(2)}) async-start(bf16[8,16,1280]{2,1,0:T(8,128)(2,1)} %bitcast.121), calls=%async_computation | async-start | bytes 655360 | tf_op jit(solution)/shard_map/all_to_all | solution.py:79
  51.8 23.6 %all-to-all-start.2 = ((bf16[8,16,1280]{2,1,0:T(8,128)(2,1)}), bf16[8,16,1280]{2,1,0:T(8,128)(2,1)S(1)}, u32[]{:S(2)}, u32[]{:S(2)}) async-start(bf16[8,16,1280]{2,1,0:T(8,128)(2,1)} %bitcast.122), calls=%async_computation.2 | async-start | bytes 655360 | tf_op jit(solution)/shard_map/all_to_all | solution.py:80
  56.7 207.0 %all-reduce.6.cloned.1.call-start = ((), (), s32[]{:S(2)}) async-start(), calls=%async_computation.13 | async-start | bytes 294912 | tf_op jit(solution)/shard_map/psum | solution.py:134
  234.3 67.2 %all-reduce.8.cloned.1.call-start = ((), (), s32[]{:S(2)}) async-start(), calls=%async_computation.14 | async-start | bytes 1179648 | tf_op jit(solution)/shard_map/psum | solution.py:98
  235.9 154.1 %reduce-scatter.6.cloned.1.call-start = ((), (), s32[]{:S(2)}) async-start(), calls=%async_computation.11 | async-start | bytes 4423680 | tf_op jit(solution)/shard_map/reduce_scatter | solution.py:155
  263.7 4.1 copy-start.5
  263.7 4.1 copy-start.6
  267.8 209.9 %reduce-scatter.8.cloned.1.call-start = ((), (), s32[]{:S(2)}) async-start(), calls=%async_computation.12 | async-start | bytes 4423680 | tf_op jit(solution)/shard_map/reduce_scatter | solution.py:158
  267.9 3.5 copy-start.9
  271.1 294.7 %reduce-scatter.4.cloned.1.call-start = ((), (), s32[]{:S(2)}) async-start(), calls=%async_computation.10 | async-start | bytes 4423680 | tf_op jit(solution)/shard_map/reduce_scatter | solution.py:152
  301.5 1.7 copy-start.4
  301.5 1.7 copy-start.7
  303.2 5.0 copy-start.8
  303.3 7.0 %copy-start.1 = (bf16[2,768,1280]{2,1,0:T(8,128)(2,1)S(1)}, bf16[2,768,1280]{2,1,0:T(8,128)(2,1)}, u32[]{:S(2)}) copy-start(bf16[2,768,1280]{2,1,0:T(8,128)(2,1)} %all-gather.4.cloned.1.call-done) | copy-start | bytes 11796484
  317.4 12.4 %all-to-all-start.3 = ((f32[8,1,16]{2,1,0:T(1,128)}), f32[8,1,16]{2,1,0:T(1,128)S(1)}, u32[]{:S(2)}, u32[]{:S(2)}) async-start(f32[8,1,16]{2,1,0:T(1,128)} %bitcast.19), calls=%async_computation.6 | async-start | bytes 8192 | tf_op jit(solution)/shard_map/all_to_all | solution.py:164
Sparse Core Ops, SparseCore 0:
  10.2 78.1 all-gather.7
  90.6 69.1 all-gather.5
  161.9 68.4 all-gather.3
  234.4 29.2 all-reduce.5
  266.9 34.6 all-reduce.7
  305.5 84.4 reduce-scatter.5
  393.7 83.9 reduce-scatter.7
  481.8 83.9 reduce-scatter.3
where the time goes:
time: 576 us; the launch traced here: 575 us
  waiting for transfers between devices  464 us (81%)
  matrix products  41.6 us (7%)
  starting transfers between devices  24.6 us (4%)
  between operations  14.4 us (2%)
  other arithmetic  12.2 us (2%)
  local copies, waits for them, and re-layouts  11.6 us (2%)
  blocking collectives  6.41 us (1%)
    reduce_scatter x1, waiting for transfers between devices, body(): lax.psum_scatter(shadow_gate.astype(jnp.bfloat16), 'ep', scatter_dimensio...  86.1 us
    reduce_scatter x1, waiting for transfers between devices, body(): lax.psum_scatter(shadow_down.astype(jnp.bfloat16), 'ep', scatter_dimensio...  85.7 us
    all_gather x1, waiting for transfers between devices, body(): lax.all_gather(up_hot, 'ep', axis=2, tiled=True)  67.5 us
    all_gather x1, waiting for transfers between devices, body(): full_down = lax.all_gather(down_hot, 'ep', axis=1, tiled=True)  66.8 us
    reduce_scatter x1, waiting for transfers between devices, body(): lax.psum_scatter(shadow_up.astype(jnp.bfloat16), 'ep', scatter_dimension=...  57.6 us
    psum x1, waiting for transfers between devices, body(): lax.psum(part_up_hot.astype(jnp.bfloat16), 'grp').astype(jnp.float32)  27.8 us
    psum x1, waiting for transfers between devices, body(): lax.psum(part_up.astype(jnp.bfloat16), 'grp').astype(jnp.float32)  26.7 us
    all_to_all x1, waiting for transfers between devices, body(): lax.all_to_all(outgoing[1], 'ep', split_axis=0, concat_axis=0, tiled=True)  13.3 us
  transfers between devices with their start and end apart: 12, of which 11 were waited for; matrix products, arithmetic and copies ran while one was open for 10% of the time, Pallas kernels for 0%

commit v1 on v0

--- a/solution.py
+++ b/solution.py
@@ -118,7 +118,12 @@
         lax.all_gather(gate_hot, "ep", axis=2, tiled=True),
         lax.all_gather(up_hot, "ep", axis=2, tiled=True),
     )
-    full_down = lax.all_gather(down_hot, "ep", axis=1, tiled=True)
+    ring = [down_hot]
+    for hop in range(7):
+        ring.append(lax.ppermute(ring[-1], "ep", [(dev, (dev + 1) % 8) for dev in range(8)]))
+    full_down = jnp.roll(
+        jnp.concatenate(ring[::-1], axis=1), (lax.axis_index("ep") + 1) * ring[0].shape[1], axis=1
+    )
     hot_weighted = (
         hot_scale.astype(jnp.float32)[:, :, None] * hot_cotan.astype(jnp.float32)
     ).astype(jnp.bfloat16)

time: 576 us -> 556 us (0.965)
  waiting for transfers between devices: 464 us -> 408 us
  starting transfers between devices: 24.6 us -> 40.4 us
  local copies, waits for them, and re-layouts: 11.6 us -> 22.1 us
  matrix products: 41.6 us -> 49.5 us
    ppermute x0 -> x7, waiting for transfers between devices: none -> 85.2 us  [body(): lax.ppermute(ring[-1], 'ep', [(dev, (dev + 1) % 8) for dev in range(8)])]
    all_gather x1 -> x0, waiting for transfers between devices: 66.8 us -> none  [body(): full_down = lax.all_gather(down_hot, 'ep', axis=1, tiled=True)]
    all_gather x1, waiting for transfers between devices: 67.5 us -> 21.6 us  [body(): lax.all_gather(up_hot, 'ep', axis=2, tiled=True)]
    unnamed x23 -> x40, local copies, waits for them, and re-layouts: 3.04 us -> 18.5 us
    all_gather x1, waiting for transfers between devices: 12.9 us -> 0.01 us  [body(): lax.all_gather(gate_hot, 'ep', axis=2, tiled=True)]
    all_to_all x1, waiting for transfers between devices: 13.3 us -> 4.56 us  [body(): lax.all_to_all(outgoing[1], 'ep', split_axis=0, concat_axis=0, tiled=True)]
    all_to_all x1, starting transfers between devices: 4.96 us -> 12.7 us  [body(): lax.all_to_all(outgoing[1], 'ep', split_axis=0, concat_axis=0, tiled=True)]
  transfers between devices with their start and end apart: 12 -> 18, of which waited for: 11 -> 15; matrix products, arithmetic and copies ran while one was open for 10% -> 13% of each run, Pallas kernels for 0% -> 0%
where the time goes in v1:
time: 556 us; the launch traced here: 554 us
  waiting for transfers between devices  408 us (73%)
  matrix products  49.5 us (9%)
  starting transfers between devices  40.4 us (7%)
  local copies, waits for them, and re-layouts  22.1 us (4%)
  between operations  14.5 us (3%)
  other arithmetic  12.9 us (2%)
  blocking collectives  6.71 us (1%)
    reduce_scatter x1, waiting for transfers between devices, body(): lax.psum_scatter(shadow_gate.astype(jnp.bfloat16), 'ep', scatter_dimensio...  86.1 us
    reduce_scatter x1, waiting for transfers between devices, body(): lax.psum_scatter(shadow_down.astype(jnp.bfloat16), 'ep', scatter_dimensio...  85.5 us
    ppermute x7, waiting for transfers between devices, body(): lax.ppermute(ring[-1], 'ep', [(dev, (dev + 1) % 8) for dev in range(8)])  85.2 us
    reduce_scatter x1, waiting for transfers between devices, body(): lax.psum_scatter(shadow_up.astype(jnp.bfloat16), 'ep', scatter_dimension=...  52.9 us
    psum x1, waiting for transfers between devices, body(): lax.psum(part_up_hot.astype(jnp.bfloat16), 'grp').astype(jnp.float32)  26.9 us
    psum x1, waiting for transfers between devices, body(): lax.psum(part_up.astype(jnp.bfloat16), 'grp').astype(jnp.float32)  26.8 us
    all_gather x1, waiting for transfers between devices, body(): lax.all_gather(up_hot, 'ep', axis=2, tiled=True)  21.6 us
    unnamed x40, local copies, waits for them, and re-layouts  18.5 us
  transfers between devices with their start and end apart: 18, of which 15 were waited for; matrix products, arithmetic and copies ran while one was open for 13% of the time, Pallas kernels for 0%

profile of v1, /device:TPU:0, one launch (start us, length us, event | category | flops | bytes accessed | tf_op | source)
XLA Modules:
  0.0 554.3 jit_solution(14156549120937686049)
XLA Ops:
  7.9 3.0 collective-permute-start
  16.9 4.9 all-to-all-start.1
  22.6 3.0 collective-permute-done
  28.1 24.1 %collective-permute-done.1 = bf16[2,96,1280]{2,1,0:T(8,128)(2,1)S(1)} collective-permute-done((bf16[2,96,1280]{2,1,0:T(8,128)(2,1)S(1)}, bf16[2,96,1280]{2,1,0:T(8,128)(2,1)S(1)}, u32[]{:S(2)}, u32[]{:S(2)}) %collective-permute-start.1) | collective-permute-done | bytes 491552 | tf_op jit(solution)/shard_map/ppermute | solution.py:123
  52.8 22.6 %collective-permute-done.2 = bf16[2,96,1280]{2,1,0:T(8,128)(2,1)} collective-permute-done((bf16[2,96,1280]{2,1,0:T(8,128)(2,1)S(1)}, bf16[2,96,1280]{2,1,0:T(8,128)(2,1)}, u32[]{:S(2)}, u32[]{:S(2)}) %collective-permute-start.2) | collective-permute-done | bytes 491552 | tf_op jit(solution)/shard_map/ppermute | solution.py:123
  79.5 21.7 %collective-permute-done.3 = bf16[2,96,1280]{2,1,0:T(8,128)(2,1)} collective-permute-done((bf16[2,96,1280]{2,1,0:T(8,128)(2,1)}, bf16[2,96,1280]{2,1,0:T(8,128)(2,1)}, u32[]{:S(2)}, u32[]{:S(2)}) %collective-permute-start.3) | collective-permute-done | bytes 491552 | tf_op jit(solution)/shard_map/ppermute | solution.py:123
  102.5 11.5 %all-to-all-start = ((bf16[8,16,1280]{2,1,0:T(8,128)(2,1)}), bf16[8,16,1280]{2,1,0:T(8,128)(2,1)S(1)}, u32[]{:S(2)}, u32[]{:S(2)}) async-start(bf16[8,16,1280]{2,1,0:T(8,128)(2,1)} %bitcast.119), calls=%async_computation | async-start | bytes 655360 | tf_op jit(solution)/shard_map/all_to_all | solution.py:79
  116.3 6.1 %collective-permute-done.4 = bf16[2,96,1280]{2,1,0:T(8,128)(2,1)} collective-permute-done((bf16[2,96,1280]{2,1,0:T(8,128)(2,1)}, bf16[2,96,1280]{2,1,0:T(8,128)(2,1)}, u32[]{:S(2)}, u32[]{:S(2)}) %collective-permute-start.4) | collective-permute-done | bytes 491552 | tf_op jit(solution)/shard_map/ppermute | solution.py:123
  122.4 11.0 %all-to-all-done = bf16[8,16,1280]{2,1,0:T(8,128)(2,1)S(1)} async-done(((bf16[8,16,1280]{2,1,0:T(8,128)(2,1)}), bf16[8,16,1280]{2,1,0:T(8,128)(2,1)S(1)}, u32[]{:S(2)}, u32[]{:S(2)}) %all-to-all-start) | async-done | bytes 327712 | tf_op jit(solution)/shard_map/all_to_all | solution.py:79
  133.4 12.7 %all-to-all-start.2 = ((bf16[8,16,1280]{2,1,0:T(8,128)(2,1)}), bf16[8,16,1280]{2,1,0:T(8,128)(2,1)S(1)}, u32[]{:S(2)}, u32[]{:S(2)}) async-start(bf16[8,16,1280]{2,1,0:T(8,128)(2,1)} %bitcast.120), calls=%async_computation.2 | async-start | bytes 655360 | tf_op jit(solution)/shard_map/all_to_all | solution.py:80
  146.1 2.7 fusion.23
  153.6 4.6 all-to-all-done.2
  159.0 7.7 %collective-permute-done.6 = bf16[2,96,1280]{2,1,0:T(8,128)(2,1)} collective-permute-done((bf16[2,96,1280]{2,1,0:T(8,128)(2,1)}, bf16[2,96,1280]{2,1,0:T(8,128)(2,1)}, u32[]{:S(2)}, u32[]{:S(2)}) %collective-permute-start.6) | collective-permute-done | bytes 491552 | tf_op jit(solution)/shard_map/ppermute | solution.py:123
  179.8 3.1 copy-done.1
  184.6 3.9 convolution_convert_fusion.10
  188.5 21.6 %all-gather.3.cloned.1.call-done = bf16[2,1280,768]{1,2,0:T(8,128)(2,1)} async-done(((bf16[2,1280,96]{1,2,0:T(8,128)(2,1)}), bf16[2,1280,768]{1,2,0:T(8,128)(2,1)}) %all-gather.3.cloned.1.call-update) | async-done | bytes 3932176 | tf_op jit(solution)/shard_map/all_gather | solution.py:119
  210.1 3.9 convolution_convert_fusion.11
  216.6 26.9 %all-reduce.6.cloned.1.call-done = (bf16[2,16,768]{2,1,0:T(8,128)(2,1)}, bf16[2,16,768]{2,1,0:T(8,128)(2,1)}, bf16[2,16,768]{2,1,0:T(8,128)(2,1)}) async-done(((bf16[2,16,768]{2,1,0:T(8,128)(2,1)}, bf16[2,16,768]{2,1,0:T(8,128)(2,1)}, bf16[2,16,768]{2,1,0:T(8,128)(2,1)}), (bf16[2,16,768]{2,1,0:T(8,128)(2,1)}, bf16[2,16,768]{2,1,0:T(8,128)(2,1)}, bf16[2,16,768]{2,1,0:T(8,128)(2,1)})) %all-reduce.6.cloned.1.call-update) | async-done | bytes 147472 | tf_op jit(solution)/shard_map/psum | solution.py:139
  243.4 4.1 convolution_convert_fusion.1
  247.6 3.2 convolution_convert_fusion
  251.1 3.1 convolution_convert_fusion.2
  254.5 26.8 %all-reduce.8.cloned.1.call-done = (bf16[128,768]{1,0:T(8,128)(2,1)}, bf16[128,768]{1,0:T(8,128)(2,1)}, bf16[128,768]{1,0:T(8,128)(2,1)}) async-done(((bf16[128,768]{1,0:T(8,128)(2,1)}, bf16[128,768]{1,0:T(8,128)(2,1)}, bf16[128,768]{1,0:T(8,128)(2,1)}), (bf16[128,768]{1,0:T(8,128)(2,1)}, bf16[128,768]{1,0:T(8,128)(2,1)}, bf16[128,768]{1,0:T(8,128)(2,1)})) %all-reduce.8.cloned.1.call-update) | async-done | bytes 589840 | tf_op jit(solution)/shard_map/psum | solution.py:98
  283.0 3.0 fusion.6
  286.0 3.0 fusion.5
  289.0 3.0 fusion.4
  292.0 3.3 fusion.29
  295.5 6.7 %all-reduce = (f32[8,1,16]{2,0,1:T(8,128)}, f32[32]{0:T(128)S(1)}) all-reduce(f32[8,1,16]{2,0,1:T(8,128)S(1)} %all_to_all.22, f32[32]{0:T(128)S(1)} %reshape.191), channel_id=1, replica_groups=mesh['grp'=4,'ep'=8] {'grp'}, use_global_device_ids=true, to_apply=%region_22.23 | all-reduce | flops 160 | bytes 1280 | tf_op jit(solution)/shard_map/psum | solution.py:168
  302.2 5.8 %all-to-all-start.3 = ((f32[8,1,16]{2,1,0:T(1,128)}), f32[8,1,16]{2,1,0:T(1,128)S(1)}, u32[]{:S(2)}, u32[]{:S(2)}) async-start(f32[8,1,16]{2,1,0:T(1,128)} %bitcast.19), calls=%async_computation.6 | async-start | bytes 8192 | tf_op jit(solution)/shard_map/all_to_all | solution.py:169
  308.1 6.2 %all-to-all-done.3 = f32[8,1,16]{2,1,0:T(1,128)S(1)} async-done(((f32[8,1,16]{2,1,0:T(1,128)}), f32[8,1,16]{2,1,0:T(1,128)S(1)}, u32[]{:S(2)}, u32[]{:S(2)}) %all-to-all-start.3) | async-done | bytes 544 | tf_op jit(solution)/shard_map/all_to_all | solution.py:169
  316.8 52.9 %reduce-scatter.6.cloned.1.call-done = bf16[2,1280,96]{1,2,0:T(8,128)(2,1)} async-done(((bf16[2,1280,768]{1,2,0:T(8,128)(2,1)}), bf16[2,1280,96]{1,2,0:T(8,128)(2,1)}) %reduce-scatter.6.cloned.1.call-update) | async-done | bytes 491536 | tf_op jit(solution)/shard_map/reduce_scatter | solution.py:160
  371.7 85.5 %reduce-scatter.8.cloned.1.call-done = bf16[2,1280,96]{1,2,0:T(8,128)(2,1)} async-done(((bf16[2,1280,768]{1,2,0:T(8,128)(2,1)}), bf16[2,1280,96]{1,2,0:T(8,128)(2,1)}) %reduce-scatter.8.cloned.1.call-update) | async-done | bytes 491536 | tf_op jit(solution)/shard_map/reduce_scatter | solution.py:163
  459.3 86.1 %reduce-scatter.4.cloned.1.call-done = bf16[2,1280,96]{1,2,0:T(8,128)(2,1)} async-done(((bf16[2,1280,768]{1,2,0:T(8,128)(2,1)}), bf16[2,1280,96]{1,2,0:T(8,128)(2,1)}) %reduce-scatter.4.cloned.1.call-update) | async-done | bytes 491536 | tf_op jit(solution)/shard_map/reduce_scatter | solution.py:157
  (120 shorter events, 52.3 us)
Async XLA Ops:
  7.2 206.9 %copy-start = (bf16[1,768,1280]{2,1,0:T(8,128)(2,1)S(1)}, bf16[1,768,1280]{2,1,0:T(8,128)(2,1)}, u32[]{:S(2)}) copy-start(bf16[1,768,1280]{2,1,0:T(8,128)(2,1)} %param.18) | copy-start | bytes 5898244
  7.2 177.5 %all-gather.5.cloned.1.call-start = ((), (), s32[]{:S(2)}) async-start(), calls=%async_computation.8 | async-start | bytes 4423680 | tf_op jit(solution)/shard_map/all_gather | solution.py:118
  7.9 17.6 %collective-permute-start = (bf16[2,96,1280]{2,1,0:T(8,128)(2,1)}, bf16[2,96,1280]{2,1,0:T(8,128)(2,1)S(1)}, u32[]{:S(2)}, u32[]{:S(2)}) collective-permute-start(bf16[2,96,1280]{2,1,0:T(8,128)(2,1)} %param.21), channel_id=1, source_target_pairs={{0,1},{1,2},{2,3},{3,4},{4,5},{5,6},{6,7},{7,0},{8,9},{9,10},{10,1... | collective-permute-start | bytes 1474568 | tf_op jit(solution)/shard_map/ppermute | solution.py:123
  16.9 85.6 %all-to-all-start.1 = ((bf16[8,1,16]{2,1,0:T(2,128)(2,1)}), bf16[8,1,16]{2,1,0:T(2,128)(2,1)S(1)}, u32[]{:S(2)}, u32[]{:S(2)}) async-start(bf16[8,1,16]{2,1,0:T(2,128)(2,1)} %all_to_all.24), calls=%async_computation.1 | async-start | bytes 8192 | tf_op jit(solution)/shard_map/all_to_all | solution.py:81
  21.8 188.3 %all-gather.3.cloned.1.call-start = ((), (), s32[]{:S(2)}) async-start(), calls=%async_computation.7 | async-start | bytes 4423680 | tf_op jit(solution)/shard_map/all_gather | solution.py:119
  25.5 49.9 %copy-start.3 = (bf16[2,96,1280]{2,1,0:T(8,128)(2,1)}, bf16[2,96,1280]{2,1,0:T(8,128)(2,1)S(1)}, u32[]{:S(2)}) copy-start(bf16[2,96,1280]{2,1,0:T(8,128)(2,1)S(1)} %collective-permute-done) | copy-start | bytes 1474564
  25.5 26.7 %collective-permute-start.1 = (bf16[2,96,1280]{2,1,0:T(8,128)(2,1)S(1)}, bf16[2,96,1280]{2,1,0:T(8,128)(2,1)S(1)}, u32[]{:S(2)}, u32[]{:S(2)}) collective-permute-start(bf16[2,96,1280]{2,1,0:T(8,128)(2,1)S(1)} %collective-permute-done), channel_id=1, source_target_pairs={{0,1},{1,2},{2,3},{3,4},{4,5},{5,6},{6,7},{7,0},{8,9},{9,10},{10,1... | collective-permute-start | bytes 1474568 | tf_op jit(solution)/shard_map/ppermute | solution.py:123
  52.2 25.2 %copy-start.5 = (bf16[2,96,1280]{2,1,0:T(8,128)(2,1)}, bf16[2,96,1280]{2,1,0:T(8,128)(2,1)S(1)}, u32[]{:S(2)}) copy-start(bf16[2,96,1280]{2,1,0:T(8,128)(2,1)S(1)} %collective-permute-done.1) | copy-start | bytes 1474564
  52.2 23.2 %collective-permute-start.2 = (bf16[2,96,1280]{2,1,0:T(8,128)(2,1)S(1)}, bf16[2,96,1280]{2,1,0:T(8,128)(2,1)}, u32[]{:S(2)}, u32[]{:S(2)}) collective-permute-start(bf16[2,96,1280]{2,1,0:T(8,128)(2,1)S(1)} %collective-permute-done.1), channel_id=1, source_target_pairs={{0,1},{1,2},{2,3},{3,4},{4,5},{5,6},{6,7},{7,0},{8,9},{9,10},{10,1... | collective-permute-start | bytes 1474568 | tf_op jit(solution)/shard_map/ppermute | solution.py:123
  75.4 25.7 %collective-permute-start.3 = (bf16[2,96,1280]{2,1,0:T(8,128)(2,1)}, bf16[2,96,1280]{2,1,0:T(8,128)(2,1)}, u32[]{:S(2)}, u32[]{:S(2)}) collective-permute-start(bf16[2,96,1280]{2,1,0:T(8,128)(2,1)} %collective-permute-done.2), channel_id=1, source_target_pairs={{0,1},{1,2},{2,3},{3,4},{4,5},{5,6},{6,7},{7,0},{8,9},{9,10},{10,1... | collective-permute-start | bytes 1474568 | tf_op jit(solution)/shard_map/ppermute | solution.py:123
  79.5 94.8 %copy-start.2 = (bf16[2,96,1280]{2,1,0:T(8,128)(2,1)S(1)}, bf16[2,96,1280]{2,1,0:T(8,128)(2,1)}, u32[]{:S(2)}) copy-start(bf16[2,96,1280]{2,1,0:T(8,128)(2,1)} %param.21) | copy-start | bytes 1474564
  101.2 21.2 %collective-permute-start.4 = (bf16[2,96,1280]{2,1,0:T(8,128)(2,1)}, bf16[2,96,1280]{2,1,0:T(8,128)(2,1)}, u32[]{:S(2)}, u32[]{:S(2)}) collective-permute-start(bf16[2,96,1280]{2,1,0:T(8,128)(2,1)} %collective-permute-done.3), channel_id=1, source_target_pairs={{0,1},{1,2},{2,3},{3,4},{4,5},{5,6},{6,7},{7,0},{8,9},{9,10},{10,1... | collective-permute-start | bytes 1474568 | tf_op jit(solution)/shard_map/ppermute | solution.py:123
  102.5 30.9 %all-to-all-start = ((bf16[8,16,1280]{2,1,0:T(8,128)(2,1)}), bf16[8,16,1280]{2,1,0:T(8,128)(2,1)S(1)}, u32[]{:S(2)}, u32[]{:S(2)}) async-start(bf16[8,16,1280]{2,1,0:T(8,128)(2,1)} %bitcast.119), calls=%async_computation | async-start | bytes 655360 | tf_op jit(solution)/shard_map/all_to_all | solution.py:79
  122.4 26.4 %collective-permute-start.5 = (bf16[2,96,1280]{2,1,0:T(8,128)(2,1)}, bf16[2,96,1280]{2,1,0:T(8,128)(2,1)}, u32[]{:S(2)}, u32[]{:S(2)}) collective-permute-start(bf16[2,96,1280]{2,1,0:T(8,128)(2,1)} %collective-permute-done.4), channel_id=1, source_target_pairs={{0,1},{1,2},{2,3},{3,4},{4,5},{5,6},{6,7},{7,0},{8,9},{9,10},{10,1... | collective-permute-start | bytes 1474568 | tf_op jit(solution)/shard_map/ppermute | solution.py:123
  133.4 24.8 %all-to-all-start.2 = ((bf16[8,16,1280]{2,1,0:T(8,128)(2,1)}), bf16[8,16,1280]{2,1,0:T(8,128)(2,1)S(1)}, u32[]{:S(2)}, u32[]{:S(2)}) async-start(bf16[8,16,1280]{2,1,0:T(8,128)(2,1)} %bitcast.120), calls=%async_computation.2 | async-start | bytes 655360 | tf_op jit(solution)/shard_map/all_to_all | solution.py:80
  146.1 97.4 %all-reduce.6.cloned.1.call-start = ((), (), s32[]{:S(2)}) async-start(), calls=%async_computation.12 | async-start | bytes 294912 | tf_op jit(solution)/shard_map/psum | solution.py:139
  148.8 17.9 %collective-permute-start.6 = (bf16[2,96,1280]{2,1,0:T(8,128)(2,1)}, bf16[2,96,1280]{2,1,0:T(8,128)(2,1)}, u32[]{:S(2)}, u32[]{:S(2)}) collective-permute-start(bf16[2,96,1280]{2,1,0:T(8,128)(2,1)} %collective-permute-done.5), channel_id=1, source_target_pairs={{0,1},{1,2},{2,3},{3,4},{4,5},{5,6},{6,7},{7,0},{8,9},{9,10},{10,1... | collective-permute-start | bytes 1474568 | tf_op jit(solution)/shard_map/ppermute | solution.py:123
  158.1 21.5 %copy-start.6 = (bf16[2,96,1280]{2,1,0:T(8,128)(2,1)S(1)}, bf16[2,96,1280]{2,1,0:T(8,128)(2,1)}, u32[]{:S(2)}) copy-start(bf16[2,96,1280]{2,1,0:T(8,128)(2,1)} %copy-done.5) | copy-start | bytes 1474564
  158.1 21.6 %copy-start.4 = (bf16[2,96,1280]{2,1,0:T(8,128)(2,1)S(1)}, bf16[2,96,1280]{2,1,0:T(8,128)(2,1)}, u32[]{:S(2)}) copy-start(bf16[2,96,1280]{2,1,0:T(8,128)(2,1)} %copy-done.3) | copy-start | bytes 1474564
  179.8 3.1 copy-start.1
  214.0 67.3 %all-reduce.8.cloned.1.call-start = ((), (), s32[]{:S(2)}) async-start(), calls=%async_computation.13 | async-start | bytes 1179648 | tf_op jit(solution)/shard_map/psum | solution.py:98
  216.5 153.2 %reduce-scatter.6.cloned.1.call-start = ((), (), s32[]{:S(2)}) async-start(), calls=%async_computation.10 | async-start | bytes 4423680 | tf_op jit(solution)/shard_map/reduce_scatter | solution.py:160
  243.4 4.2 copy-start.8
  243.4 4.2 copy-start.9
  243.4 7.7 %copy-start.10 = (bf16[2,16,768]{2,1,0:T(8,128)(2,1)S(1)}, bf16[2,16,768]{2,1,0:T(8,128)(2,1)}, u32[]{:S(2)}) copy-start(bf16[2,16,768]{2,1,0:T(8,128)(2,1)} %get-tuple-element.37) | copy-start | bytes 147460
  247.6 209.7 %reduce-scatter.8.cloned.1.call-start = ((), (), s32[]{:S(2)}) async-start(), calls=%async_computation.11 | async-start | bytes 4423680 | tf_op jit(solution)/shard_map/reduce_scatter | solution.py:163
  250.9 294.6 %reduce-scatter.4.cloned.1.call-start = ((), (), s32[]{:S(2)}) async-start(), calls=%async_computation.9 | async-start | bytes 4423680 | tf_op jit(solution)/shard_map/reduce_scatter | solution.py:157
  281.3 7.8 %copy-start.7 = (bf16[128,768]{1,0:T(8,128)(2,1)S(1)}, bf16[128,768]{1,0:T(8,128)(2,1)}, u32[]{:S(2)}) copy-start(bf16[128,768]{1,0:T(8,128)(2,1)} %get-tuple-element.41) | copy-start | bytes 589828
  302.2 12.2 %all-to-all-start.3 = ((f32[8,1,16]{2,1,0:T(1,128)}), f32[8,1,16]{2,1,0:T(1,128)S(1)}, u32[]{:S(2)}, u32[]{:S(2)}) async-start(f32[8,1,16]{2,1,0:T(1,128)} %bitcast.19), calls=%async_computation.6 | async-start | bytes 8192 | tf_op jit(solution)/shard_map/all_to_all | solution.py:169
Sparse Core Ops, SparseCore 0:
  10.2 98.9 all-gather.4
  111.4 98.6 all-gather.2
  214.1 29.2 all-reduce.5
  246.6 34.6 all-reduce.7
  285.2 84.4 reduce-scatter.5
  373.2 83.9 reduce-scatter.7
  461.4 83.9 reduce-scatter.3
